TPU v7x, 512 devices: a whole 4x8x8 slice. The times are simulated.
512 devices in a mesh: rows: 32 (over y, x), vocab: 16 (over z, core).
Axes of the slice: x: 4, y: 8, z: 8, core: 2. Of those that a mesh axis runs over, the one named last changes fastest.
Arguments:
- hidden: bfloat16 [12288, 8192], P('rows', 'vocab'), may hold values from -128 to 128
- head: bfloat16 [8192, 8192], P('rows', 'vocab'), may hold values from -4 to 4
- targets: int32 [12288], P('rows'), may hold values from 0 to 128255
- live: int32 [12288], P('rows'), may hold values from 0 to 1, as said below
- prior_lse: float32 [12288], P('rows'), may hold values from 10 to 18
- prior_mean: float32 [12288], P('rows'), may hold values from 2 to 8
- prior_target: float32 [12288], P('rows'), may hold values from -12 to 12
- seq_lengths: int32 [32], replicated, may hold values from 1 to 768, 12288 in all
Outputs:
- logprob: float32 [12288], P(('rows', 'vocab'))
- entropy: float32 [12288], P(('rows', 'vocab'))
- seq_score: float32 [32], replicated
Inputs may be any that keep to these rules, and one draw needn't show every extreme that they name: Within the 384 rows of each index of rows, the live rows come first; every such index has at least 48 live rows and some index has all 384.
All inputs are finite; a program needn't handle non-finite values.
Results may differ from a plain program's by a relative error of at most 0.0003.
Values may be sent and summed in bfloat16 or wider, within the bound.
No kernel may reach another device: no remote copies, remote signals or barrier semaphores. Data moves between devices by JAX's collectives and lax.ppermute only.
A program may use at most 64 MiB of HBM per device.

v0:
```python
import jax
import jax.numpy as jnp
from jax import lax
from jax.sharding import PartitionSpec as P

VOCAB = 128256
SEQS = 32
GSIZE = 8


def finish_rows(block_peak, block_mass, block_moment, block_target, live, prior_lse, prior_mean):
    highest = jnp.maximum(block_peak, prior_lse)
    earlier = jnp.exp(prior_lse - highest)
    scaled = jnp.exp(block_peak - highest)
    total_mass = earlier + block_mass * scaled
    norm_log = highest + jnp.log(total_mass)
    average = (earlier * prior_mean + scaled * block_moment) / total_mass
    keeping = live.astype(jnp.float32)
    return (keeping * (block_target - norm_log), keeping * (norm_log - average))


def local(hidden, head, targets, live, prior_lse, prior_mean, prior_target, seq_lengths):
    rows_here = hidden.shape[0]
    cols_here = head.shape[1]
    spread = lax.axis_size("vocab")
    which = lax.axis_index("vocab")
    block_first = VOCAB - cols_here * spread
    first_col = block_first + which * cols_here
    gathered = lax.all_gather(hidden, "vocab", axis=1, tiled=True)
    logits = jnp.dot(
        gathered,
        lax.all_gather(head, "rows", axis=0, tiled=True),
        preferred_element_type=jnp.float32,
    )
    row_peak = jnp.max(logits, axis=1)
    weights = jnp.exp(logits - row_peak[:, None])
    row_mass = jnp.sum(weights, axis=1)
    moment = jnp.sum(weights * logits, axis=1)
    column = targets - first_col
    columns = lax.broadcasted_iota(jnp.int32, logits.shape, 1)
    picked = jnp.sum(jnp.where(columns == column[:, None], logits, jnp.zeros_like(logits)), axis=1)
    stats = jnp.stack([row_peak, row_mass, moment, picked])
    every = lax.all_gather(stats, "vocab", axis=0, tiled=False)
    peaks = every[:, 0]
    highest = jnp.max(peaks, axis=0)
    factor = jnp.exp(peaks - highest[None, :])
    mass_all = jnp.sum(every[:, 1] * factor, axis=0)
    moment_all = jnp.sum(every[:, 2] * factor, axis=0)
    picked_all = jnp.sum(every[:, 3], axis=0)
    block_target = jnp.where(targets >= block_first, picked_all, prior_target)
    logprob, entropy = finish_rows(
        highest, mass_all, moment_all, block_target, live, prior_lse, prior_mean
    )
    share = rows_here // spread
    begin = which * share
    logprob_share = lax.dynamic_slice_in_dim(logprob, begin, share, 0)
    entropy_share = lax.dynamic_slice_in_dim(entropy, begin, share, 0)
    global_rows = lax.axis_index("rows") * rows_here + jnp.arange(rows_here, dtype=jnp.int32)
    endings = jnp.cumsum(seq_lengths)
    member = jnp.sum((global_rows[:, None] >= endings[None, :]).astype(jnp.int32), axis=1)
    onehot = (member[:, None] == jnp.arange(SEQS, dtype=jnp.int32)[None, :]).astype(jnp.float32)
    partial_sums = jnp.sum(onehot * logprob[:, None], axis=0)
    sums = jnp.sum(lax.all_gather(partial_sums, "rows", axis=0, tiled=False), axis=0)
    seq_mean = sums / seq_lengths.astype(jnp.float32)
    grouped = seq_mean.reshape(SEQS // GSIZE, GSIZE)
    seq_score = (grouped - jnp.mean(grouped, axis=1, keepdims=True)).reshape(SEQS)
    return (logprob_share, entropy_share, seq_score)


def solution(mesh):
    return jax.shard_map(
        local,
        mesh=mesh,
        in_specs=(
            P("rows", "vocab"),
            P("rows", "vocab"),
            P("rows"),
            P("rows"),
            P("rows"),
            P("rows"),
            P("rows"),
            P(),
        ),
        out_specs=(P(("rows", "vocab")), P(("rows", "vocab")), P()),
        check_vma=False,
    )
```

profile of v0, /device:TPU:2, one launch (start us, length us, event | category | flops | bytes accessed | tf_op | source)
XLA Modules:
  0.0 275.6 jit_solution(6936003982868174059)
XLA Ops:
  7.2 0.7 all-gather.6.cloned.1.call-update
  7.9 0.7 all-gather.8.cloned.1.call-update
  8.7 0.7 copy.22
  9.5 0.1 reduce.2
  9.6 1.3 dynamic-slice
  11.5 0.1 convert_reduce_fusion
  11.6 0.7 broadcast_subtract_fusion
  12.3 52.0 %all-gather.6.cloned.1.call-done = bf16[384,8192]{1,0:T(8,128)(2,1)} async-done(((bf16[384,512]{1,0:T(8,128)(2,1)}), bf16[384,8192]{1,0:T(8,128)(2,1)}) %all-gather.6.cloned.1.call-update) | async-done | bytes 6291472 | tf_op jit(solution)/shard_map/all_gather | solution.py:29
  64.3 103.5 %all-gather.8.cloned.1.call-done = bf16[8192,512]{1,0:T(8,128)(2,1)} async-done(((bf16[256,512]{1,0:T(8,128)(2,1)}), bf16[8192,512]{1,0:T(8,128)(2,1)}) %all-gather.8.cloned.1.call-update) | async-done | bytes 8388624 | tf_op jit(solution)/shard_map/all_gather | solution.py:32
  167.7 8.0 %fusion.7 = (f32[384]{0:T(512)S(1)}, f32[384,512]{1,0:T(8,128)S(1)}) fusion(bf16[384,8192]{1,0:T(8,128)(2,1)} %all-gather.6.cloned.1.call-done, bf16[8192,512]{1,0:T(8,128)(2,1)} %all-gather.8.cloned.1.call-done), kind=kOutput, calls=%fused_computation.30 | convolution fusion | flops 3221421568 | bytes 15468032 | tf_op jit(solution)/shard_map/dot_general | solution.py:30
  175.8 0.5 fusion
  176.3 18.3 %all-gather.2 = f32[16,4,384]{2,1,0:T(4,128)S(1)} all-gather(f32[1,4,384]{2,1,0:T(4,128)S(1)} %maximum_bitcast_fusion), channel_id=2, replica_groups=mesh['rows'=32,'vocab'=16] {'vocab'}, dimensions={0}, use_global_device_ids=true | all-gather | bytes 104448 | tf_op jit(solution)/shard_map/all_gather | solution.py:43
  194.6 0.1 fusion.6
  194.8 0.6 dynamic_slice.6
  195.4 0.6 dynamic_slice.7
  196.0 0.1 select_reduce_fusion.1
  196.1 0.2 dynamic-update-slice
  196.4 71.4 %all-reduce = f32[1024]{0:T(1024)S(1)} all-reduce(f32[1024]{0:T(1024)S(1)} %dynamic-update-slice), channel_id=3, replica_groups=mesh['rows'=32,'vocab'=16] {'rows'}, use_global_device_ids=true, to_apply=%add | all-reduce | flops 1024 | bytes 8192
  267.8 0.1 reshape.52
  267.9 0.1 reshape.50
  268.0 0.1 reduce_sum.99
  268.1 0.1 sub.55
  268.2 0.1 sub.56
  268.2 0.5 sub.57
  (27 shorter events, 0.3 us)
Async XLA Ops:
  7.2 57.1 %all-gather.6.cloned.1.call-start = ((), (), s32[]{:S(2)}) async-start(), calls=%async_computation | async-start | bytes 6684672 | tf_op jit(solution)/shard_map/all_gather | solution.py:29
  7.9 159.8 %all-gather.8.cloned.1.call-start = ((), (), s32[]{:S(2)}) async-start(), calls=%async_computation.1 | async-start | bytes 8650752 | tf_op jit(solution)/shard_map/all_gather | solution.py:32
  12.3 182.5 %copy-start = (s32[384]{0:T(512)S(1)}, s32[384]{0:T(512)}, u32[]{:S(2)}) copy-start(s32[384]{0:T(512)} %param.10) | copy-start | bytes 4612
  12.3 182.5 %copy-start.1 = (f32[384]{0:T(512)S(1)}, f32[384]{0:T(512)}, u32[]{:S(2)}) copy-start(f32[384]{0:T(512)} %param.13) | copy-start | bytes 4612
  12.3 182.5 %copy-start.2 = (s32[384]{0:T(512)S(1)}, s32[384]{0:T(512)}, u32[]{:S(2)}) copy-start(s32[384]{0:T(512)} %param.11) | copy-start | bytes 4612
  12.3 182.5 %copy-start.3 = (f32[384]{0:T(512)S(1)}, f32[384]{0:T(512)}, u32[]{:S(2)}) copy-start(f32[384]{0:T(512)} %param.12) | copy-start | bytes 4612
  12.3 182.5 %copy-start.4 = (f32[384]{0:T(512)S(1)}, f32[384]{0:T(512)}, u32[]{:S(2)}) copy-start(f32[384]{0:T(512)} %param.14) | copy-start | bytes 4612
  12.3 255.5 %copy-start.5 = (s32[32]{0:T(128)S(1)}, s32[32]{0:T(128)}, u32[]{:S(2)}) copy-start(s32[32]{0:T(128)} %param.15) | copy-start | bytes 388
Sparse Core Ops, SparseCore 0:
  10.1 54.0 all-gather.5
  67.4 100.2 all-gather.7
where the time goes:
time: 276 us
  waiting for transfers between devices  157 us (57%)
  blocking collectives  89.7 us (32%)
  between operations  14.8 us (5%)
  matrix products  8 us (3%)
  local copies, waits for them, and re-layouts  3.78 us (1%)
    all_gather x1, waiting for transfers between devices, local(): lax.all_gather(head, 'rows', axis=0, tiled=True)  103 us
    unnamed x1, blocking collectives  71.4 us
    all_gather x1, waiting for transfers between devices, local(): gathered = lax.all_gather(hidden, 'vocab', axis=1, tiled=True)  52 us
    all_gather x1, blocking collectives, local(): every = lax.all_gather(stats, 'vocab', axis=0, tiled=False)  18.3 us
    dot_general x1, matrix products, local(): jnp.dot(gathered, lax.all_gather(head, 'rows', axis=0, tiled=True), prefe...  8 us
  transfers between devices with their start and end apart: 2, of which 2 were waited for; matrix products, arithmetic and copies ran while one was open for 1% of the time, Pallas kernels for 0%

commit v1 on v0

--- a/solution.py
+++ b/solution.py
@@ -6,6 +6,11 @@
 VOCAB = 128256
 SEQS = 32
 GSIZE = 8
+
+
+def gather_over(shard, name, dim):
+    sent = jnp.stack([shard] * lax.axis_size(name))
+    return jnp.concatenate(lax.all_to_all(sent, name, 0, 0), axis=dim)
 
 
 def finish_rows(block_peak, block_mass, block_moment, block_target, live, prior_lse, prior_mean):
@@ -27,11 +32,7 @@
     block_first = VOCAB - cols_here * spread
     first_col = block_first + which * cols_here
     gathered = lax.all_gather(hidden, "vocab", axis=1, tiled=True)
-    logits = jnp.dot(
-        gathered,
-        lax.all_gather(head, "rows", axis=0, tiled=True),
-        preferred_element_type=jnp.float32,
-    )
+    logits = jnp.dot(gathered, gather_over(head, "rows", 0), preferred_element_type=jnp.float32)
     row_peak = jnp.max(logits, axis=1)
     weights = jnp.exp(logits - row_peak[:, None])
     row_mass = jnp.sum(weights, axis=1)

time: 276 us -> 333 us (1.21)
  the two profiles are of different devices: /device:TPU:2 before, /device:TPU:32 now
where the time goes in v1:
time: 333 us; the launch traced here: 332 us
  waiting for transfers between devices  183 us (55%)
  blocking collectives  106 us (32%)
  between operations  14.8 us (4%)
  starting transfers between devices  10.3 us (3%)
  local copies, waits for them, and re-layouts  8.22 us (2%)
  matrix products  8.04 us (2%)
    all_to_all x1, waiting for transfers between devices, gather_over(): return jnp.concatenate(lax.all_to_all(sent, name, 0, 0), axis=dim)  129 us
    unnamed x1, blocking collectives  83.6 us
    all_gather x1, waiting for transfers between devices, local(): gathered = lax.all_gather(hidden, 'vocab', axis=1, tiled=True)  53.4 us
    all_gather x1, blocking collectives, local(): every = lax.all_gather(stats, 'vocab', axis=0, tiled=False)  22.7 us
    all_to_all x1, starting transfers between devices, gather_over(): return jnp.concatenate(lax.all_to_all(sent, name, 0, 0), axis=dim)  10.3 us
    dot_general x1, matrix products, local(): jnp.dot(gathered, gather_over(head, 'rows', 0), preferred_element_type=jn...  8.04 us
  transfers between devices with their start and end apart: 2, of which 2 were waited for; matrix products, arithmetic and copies ran while one was open for 0% of the time, Pallas kernels for 0%

profile of v1, /device:TPU:32, one launch (start us, length us, event | category | flops | bytes accessed | tf_op | source)
XLA Modules:
  0.0 332.4 jit_solution(10693106749679313728)
XLA Ops:
  7.2 5.1 %stack.12 = bf16[32,256,512]{2,1,0:T(8,128)(2,1)} broadcast(bf16[256,512]{1,0:T(8,128)(2,1)} %param.9), dimensions={1,2} | broadcast | bytes 8650752 | tf_op jit(solution)/shard_map/stack | solution.py:12
  12.3 10.3 %all-to-all-start = ((bf16[32,256,512]{2,1,0:T(8,128)(2,1)}), bf16[32,256,512]{2,1,0:T(8,128)(2,1)}, u32[]{:S(2)}, u32[]{:S(2)}) async-start(bf16[32,256,512]{2,1,0:T(8,128)(2,1)} %stack.12), calls=%async_computation | async-start | bytes 16777216 | tf_op jit(solution)/shard_map/all_to_all | solution.py:13
  22.6 0.7 all-gather.5.cloned.1.call-update
  23.3 0.1 copy.22
  23.4 0.1 reduce.2
  23.6 1.3 dynamic-slice
  25.5 0.1 convert_reduce_fusion
  25.6 53.4 %all-gather.5.cloned.1.call-done = bf16[384,8192]{1,0:T(8,128)(2,1)} async-done(((bf16[384,512]{1,0:T(8,128)(2,1)}), bf16[384,8192]{1,0:T(8,128)(2,1)}) %all-gather.5.cloned.1.call-update) | async-done | bytes 6291472 | tf_op jit(solution)/shard_map/all_gather | solution.py:34
  79.0 128.8 %all-to-all-done = bf16[32,256,512]{2,1,0:T(8,128)(2,1)} async-done(((bf16[32,256,512]{2,1,0:T(8,128)(2,1)}), bf16[32,256,512]{2,1,0:T(8,128)(2,1)}, u32[]{:S(2)}, u32[]{:S(2)}) %all-to-all-start) | async-done | bytes 8388640 | tf_op jit(solution)/shard_map/all_to_all | solution.py:13
  207.9 8.0 %fusion.7 = (f32[384]{0:T(512)S(1)}, f32[384,512]{1,0:T(8,128)S(1)}) fusion(bf16[384,8192]{1,0:T(8,128)(2,1)} %all-gather.5.cloned.1.call-done, bf16[8192,512]{1,0:T(8,128)(2,1)} %bitcast), kind=kOutput, calls=%fused_computation.30 | convolution fusion | flops 3221421568 | bytes 15468032 | tf_op jit(solution)/shard_map/dot_general | solution.py:35
  215.9 0.5 fusion
  216.5 22.7 %all-gather.2 = f32[16,4,384]{2,1,0:T(4,128)S(1)} all-gather(f32[1,4,384]{2,1,0:T(4,128)S(1)} %maximum_bitcast_fusion), channel_id=2, replica_groups=mesh['rows'=32,'vocab'=16] {'vocab'}, dimensions={0}, use_global_device_ids=true | all-gather | bytes 104448 | tf_op jit(solution)/shard_map/all_gather | solution.py:44
  239.2 0.1 fusion.6
  239.4 0.1 select_reduce_fusion.1
  239.5 0.2 dynamic-update-slice
  239.8 83.6 %all-reduce = f32[1024]{0:T(1024)S(1)} all-reduce(f32[1024]{0:T(1024)S(1)} %dynamic-update-slice), channel_id=3, replica_groups=mesh['rows'=32,'vocab'=16] {'rows'}, use_global_device_ids=true, to_apply=%add | all-reduce | flops 1024 | bytes 8192
  323.4 0.1 reshape.58
  323.5 0.1 reshape.56
  323.6 0.1 reduce_sum.99
  323.7 0.1 sub.55
  323.8 0.1 sub.56
  323.8 0.5 sub.57
  324.4 0.6 dynamic_slice.6
  325.0 0.6 dynamic_slice.7
  (27 shorter events, 0.2 us)
Async XLA Ops:
  12.3 11.0 %copy-start.5 = (s32[32]{0:T(128)S(1)}, s32[32]{0:T(128)}, u32[]{:S(2)}) copy-start(s32[32]{0:T(128)} %param.15) | copy-start | bytes 388
  12.3 13.3 %copy-start = (s32[384]{0:T(512)S(1)}, s32[384]{0:T(512)}, u32[]{:S(2)}) copy-start(s32[384]{0:T(512)} %param.10) | copy-start | bytes 4612
  12.3 195.6 %all-to-all-start = ((bf16[32,256,512]{2,1,0:T(8,128)(2,1)}), bf16[32,256,512]{2,1,0:T(8,128)(2,1)}, u32[]{:S(2)}, u32[]{:S(2)}) async-start(bf16[32,256,512]{2,1,0:T(8,128)(2,1)} %stack.12), calls=%async_computation | async-start | bytes 16777216 | tf_op jit(solution)/shard_map/all_to_all | solution.py:13
  22.5 56.5 %all-gather.5.cloned.1.call-start = ((), (), s32[]{:S(2)}) async-start(), calls=%async_computation.1 | async-start | bytes 6684672 | tf_op jit(solution)/shard_map/all_gather | solution.py:34
  207.9 31.5 %copy-start.1 = (f32[384]{0:T(512)S(1)}, f32[384]{0:T(512)}, u32[]{:S(2)}) copy-start(f32[384]{0:T(512)} %param.13) | copy-start | bytes 4612
  207.9 31.5 %copy-start.2 = (s32[384]{0:T(512)S(1)}, s32[384]{0:T(512)}, u32[]{:S(2)}) copy-start(s32[384]{0:T(512)} %param.11) | copy-start | bytes 4612
  207.9 31.5 %copy-start.3 = (f32[384]{0:T(512)S(1)}, f32[384]{0:T(512)}, u32[]{:S(2)}) copy-start(f32[384]{0:T(512)} %param.12) | copy-start | bytes 4612
  207.9 31.5 %copy-start.4 = (f32[384]{0:T(512)S(1)}, f32[384]{0:T(512)}, u32[]{:S(2)}) copy-start(f32[384]{0:T(512)} %param.14) | copy-start | bytes 4612
Sparse Core Ops, SparseCore 0:
  25.5 53.4 all-gather.4
